TPU v7x, 32 devices: a whole 2x2x4 slice. The times are simulated.
32 devices in a mesh: groups: 2 (over x), blk: 16 (over z, y, core).
Axes of the slice: x: 2, y: 2, z: 4, core: 2. Of those that a mesh axis runs over, the one named last changes fastest.
Arguments:
- layer_input_tokens: bfloat16 [384, 8192], P('groups', 'blk'), parts along dimension 0, may hold values from -6 to 6
- input_norm_gain: float32 [8192], replicated, may hold values from 0.5 to 1.5
- query_weight: bfloat16 [8192, 8192], P(None, 'blk'), may hold values from -0.0625 to 0.0625
- key_value_weight: bfloat16 [8192, 2048], P(None, 'blk'), may hold values from -0.0625 to 0.0625
- output_weight: bfloat16 [8192, 8192], P(None, 'blk'), may hold values from -0.5 to 0.5
- adapter_down_weight: bfloat16 [16, 64, 8192], P('blk'), may hold values from -0.0625 to 0.0625
- adapter_up_weight: bfloat16 [16, 64, 8192], P(None, None, 'blk'), may hold values from -0.75 to 0.75
- key_value_page_pool: bfloat16 [512, 128, 2048], P(('groups', 'blk')), parts along dimension 0, may hold values from -240 to 240
- request_adapter: int32 [128], P('groups'), parts along dimension 0, may hold values from 0 to 15
- adapter_storage_slot: int32 [16], replicated, may hold values from 0 to 15, each once
- cached_lengths: int32 [128], P('groups'), parts along dimension 0, may hold values from 1 to 512, as said below
- request_page_tables: int32 [128, 4], P('groups'), parts along dimension 0, may hold values from -1 to 255, as said below
Outputs:
- layer_out: bfloat16 [384, 8192], P('groups', 'blk'), parts along dimension 0
There are 2 independent parts, one for each index of `groups`. A program takes and returns all parts, laid end to end along the dimension named above; an argument that names none is the same for every part. Nothing has to cross between parts.
Inputs may be any that keep to these rules, and one draw needn't show every extreme that they name: `cached_lengths`: each request's cached length; the longest is exactly 512. `request_page_tables`: row r holds ceil(cached_lengths[r] / 128) page numbers first and -1 after them; no page is named twice in the whole table.
All inputs are finite; a program needn't handle non-finite values.
Results may differ from a plain program's by a relative error of at most 0.0085.
The roundings to bfloat16 on the way count: a program that leaves them out, or rounds other values in their place, can miss the bound.
Values may be sent and summed in bfloat16 or wider, within the bound.
No kernel may reach another device: no remote copies, remote signals or barrier semaphores. Data moves between devices by JAX's collectives and lax.ppermute only.
A program may use at most 128 MiB of HBM per device.

v0:
```python
import math
import jax
import jax.numpy as jnp
from jax import lax
from jax.sharding import PartitionSpec as P

QUERY_HEADS = 64
KEY_VALUE_HEADS = 8
HEAD_WIDTH = 128
PAGE_LENGTH = 128
NEW_TOKENS = 3
theta_base = 500000.0
neg_large = -1e30


def apply_rotation(values, token_positions, first_col, rot_limit):
    width_cols = values.shape[1]
    columns = first_col + jnp.arange(width_cols, dtype=jnp.int32)
    pair_index = (columns % HEAD_WIDTH // 2).astype(jnp.float32)
    inverse = jnp.exp(pair_index * (-2.0 * math.log(theta_base) / HEAD_WIDTH))
    angles = token_positions[:, None] * inverse[None, :]
    cos_val = jnp.cos(angles[:, 0::2])
    sine_val = jnp.sin(angles[:, 0::2])
    even_part = values[:, 0::2]
    odd_part = values[:, 1::2]
    turned = jnp.stack(
        [even_part * cos_val - odd_part * sine_val, even_part * sine_val + odd_part * cos_val],
        axis=-1,
    ).reshape(values.shape)
    return jnp.where((columns < rot_limit)[None, :], turned, values)


def normalize(layer_input_tokens, input_norm_gain):
    values = layer_input_tokens.astype(jnp.float32)
    mean_square = jnp.mean(values * values, axis=-1, keepdims=True)
    return (values * lax.rsqrt(mean_square + 1e-05) * input_norm_gain[None, :]).astype(jnp.bfloat16)


def positions_of(cached_lengths):
    steps_row = jnp.arange(NEW_TOKENS, dtype=jnp.int32)
    return (
        jnp.repeat(cached_lengths, NEW_TOKENS) + jnp.tile(steps_row, cached_lengths.shape[0])
    ).astype(jnp.float32)


def to_tokens(request_first_layout):
    request_count = request_first_layout.shape[0]
    trailing_shape = request_first_layout.shape[3:]
    query_group_width = QUERY_HEADS // KEY_VALUE_HEADS
    split_head_shape = request_first_layout.reshape(
        (request_count, KEY_VALUE_HEADS, NEW_TOKENS, query_group_width) + trailing_shape
    )
    order_axes = (0, 2, 1, 3) + tuple(range(4, 4 + len(trailing_shape)))
    return split_head_shape.transpose(order_axes).reshape(request_count * NEW_TOKENS, -1)


def local(
    layer_input_tokens,
    input_norm_gain,
    query_weight,
    key_value_weight,
    output_weight,
    adapter_down_weight,
    adapter_up_weight,
    key_value_page_pool,
    request_adapter,
    adapter_storage_slot,
    cached_lengths,
    request_page_tables,
):
    own_index = lax.axis_index("blk")
    gathered = lax.all_gather(layer_input_tokens, "blk", axis=1, tiled=True)
    normalized_input = normalize(gathered, input_norm_gain)
    request_count = cached_lengths.shape[0]
    adapter_total = adapter_storage_slot.shape[0]
    choose = request_adapter[:, None] == jnp.arange(adapter_total, dtype=jnp.int32)[None, :]
    req_slot = jnp.sum(jnp.where(choose, adapter_storage_slot[None, :], 0), axis=1)
    token_cache_slot = jnp.repeat(req_slot, NEW_TOKENS)
    local_token_count = adapter_down_weight.shape[0]
    local_pick = (
        token_cache_slot[:, None] - own_index * local_token_count
        == jnp.arange(local_token_count, dtype=jnp.int32)[None, :]
    )
    output_projected = jnp.einsum(
        "ly,mxy->lmx", normalized_input, adapter_down_weight, preferred_element_type=jnp.float32
    )
    partial_codes = jnp.sum(jnp.where(local_pick[:, :, None], output_projected, 0.0), axis=1)
    adapter_choice_index = lax.psum(partial_codes, "blk").astype(jnp.bfloat16)
    up_weight_rows = adapter_up_weight[token_cache_slot]
    adapter_query_update = jnp.einsum(
        "gk,gkq->gq", adapter_choice_index, up_weight_rows, preferred_element_type=jnp.float32
    )
    token_positions = positions_of(cached_lengths)
    query_cols = query_weight.shape[1]
    keyval_cols = key_value_weight.shape[1]
    query_part = apply_rotation(
        jnp.dot(normalized_input, query_weight, preferred_element_type=jnp.float32)
        + adapter_query_update,
        token_positions,
        own_index * query_cols,
        QUERY_HEADS * HEAD_WIDTH,
    ).astype(jnp.bfloat16)
    keyval_part = apply_rotation(
        jnp.dot(normalized_input, key_value_weight, preferred_element_type=jnp.float32),
        token_positions,
        own_index * keyval_cols,
        KEY_VALUE_HEADS * HEAD_WIDTH,
    ).astype(jnp.bfloat16)
    query_vectors, key_value_rows = (
        lax.all_gather(query_part, "blk", axis=1, tiled=True),
        lax.all_gather(keyval_part, "blk", axis=1, tiled=True),
    )
    query_group_width = QUERY_HEADS // KEY_VALUE_HEADS
    query_feature_width = query_group_width * NEW_TOKENS
    score_scale = 1.0 / math.sqrt(HEAD_WIDTH)
    query_req = (
        query_vectors.reshape(
            request_count, NEW_TOKENS, KEY_VALUE_HEADS, query_group_width, HEAD_WIDTH
        )
        .transpose(0, 2, 1, 3, 4)
        .reshape(request_count, KEY_VALUE_HEADS, query_feature_width, HEAD_WIDTH)
    )
    fresh_token_rows = key_value_rows.reshape(
        request_count, NEW_TOKENS, 2, KEY_VALUE_HEADS, HEAD_WIDTH
    )
    request_page_count = key_value_page_pool.shape[0]
    table_width = request_page_tables.shape[1]
    page_ids = own_index * request_page_count + jnp.arange(request_page_count, dtype=jnp.int32)
    matches = request_page_tables[None, :, :] == page_ids[:, None, None]
    page_owner = jnp.any(matches, axis=2)
    page_live = jnp.any(page_owner, axis=1)
    page_req = jnp.sum(
        jnp.where(page_owner, jnp.arange(request_count, dtype=jnp.int32)[None, :], 0), axis=1
    )
    page_slot = jnp.sum(
        jnp.where(matches, jnp.arange(table_width, dtype=jnp.int32)[None, None, :], 0), axis=(1, 2)
    )
    page_len = jnp.sum(jnp.where(page_owner, cached_lengths[None, :], 0), axis=1)
    key_pos = page_slot[:, None] * PAGE_LENGTH + jnp.arange(PAGE_LENGTH, dtype=jnp.int32)[None, :]
    key_valid = page_live[:, None] & (key_pos < page_len[:, None])
    valid_full = key_valid[:, None, None, :]
    gathered_cache_pages = key_value_page_pool.reshape(
        request_page_count, PAGE_LENGTH, 2, KEY_VALUE_HEADS, HEAD_WIDTH
    )
    query_page = query_req[page_req]
    scores = (
        jnp.einsum(
            "skqd,spkd->skqp",
            query_page,
            gathered_cache_pages[:, :, 0],
            preferred_element_type=jnp.float32,
        )
        * score_scale
    )
    masked = jnp.where(valid_full, scores, neg_large)
    page_peak = jnp.max(masked, axis=-1)
    req_peak = jnp.max(
        jnp.where(page_owner[:, :, None, None], page_peak[:, None], neg_large), axis=0
    )
    fresh_scores = (
        jnp.einsum(
            "rkqd,rjkd->rkqj",
            query_req,
            fresh_token_rows[:, :, 0],
            preferred_element_type=jnp.float32,
        )
        * score_scale
    )
    step_of = jnp.arange(query_feature_width, dtype=jnp.int32) // query_group_width
    fresh_ok = (jnp.arange(NEW_TOKENS, dtype=jnp.int32)[None, :] <= step_of[:, None])[None, None]
    fresh_masked = jnp.where(fresh_ok, fresh_scores, neg_large)
    top_score = lax.pmax(jnp.maximum(req_peak, jnp.max(fresh_masked, axis=-1)), "blk")
    weights = jnp.where(valid_full, jnp.exp(masked - top_score[page_req][..., None]), 0.0)
    page_num = jnp.einsum(
        "skqp,spkd->skqd",
        weights.astype(jnp.bfloat16),
        gathered_cache_pages[:, :, 1],
        preferred_element_type=jnp.float32,
    )
    owner_frac = page_owner.astype(jnp.float32)
    req_num = jnp.einsum("sr,skqd->rkqd", owner_frac, page_num, precision=lax.Precision.HIGHEST)
    req_den = jnp.einsum(
        "sr,skq->rkq", owner_frac, jnp.sum(weights, axis=-1), precision=lax.Precision.HIGHEST
    )
    fresh_weights = jnp.where(fresh_ok, jnp.exp(fresh_masked - top_score[..., None]), 0.0)
    fresh_num = jnp.einsum(
        "rkqj,rjkd->rkqd",
        fresh_weights.astype(jnp.bfloat16),
        fresh_token_rows[:, :, 1],
        preferred_element_type=jnp.float32,
    )
    fresh_den = jnp.sum(fresh_weights, axis=-1)
    num_tok = to_tokens(req_num)
    den_tok = to_tokens(req_den[..., None])
    fresh_num_tok = to_tokens(fresh_num)
    fresh_den_tok = to_tokens(fresh_den[..., None])
    num_all, den_all = lax.psum((num_tok, den_tok), "blk")
    totals = den_all + fresh_den_tok
    attended = ((num_all + fresh_num_tok) / jnp.repeat(totals, HEAD_WIDTH, axis=1)).astype(
        jnp.bfloat16
    )
    return jnp.dot(attended, output_weight, preferred_element_type=jnp.float32).astype(jnp.bfloat16)


def solution(mesh):
    placed = (
        P("groups", "blk"),
        P(),
        P(None, "blk"),
        P(None, "blk"),
        P(None, "blk"),
        P("blk", None, None),
        P(None, None, "blk"),
        P(("groups", "blk"), None, None),
        P("groups"),
        P(),
        P("groups"),
        P("groups", None),
    )
    return jax.shard_map(
        local, mesh=mesh, in_specs=placed, out_specs=P("groups", "blk"), check_vma=False
    )
```

profile of v0, /device:TPU:0, one launch (start us, length us, event | category | flops | bytes accessed | tf_op | source)
XLA Modules:
  0.0 457.9 jit_solution(6853859499092122322)
XLA Ops:
  6.5 0.7 all-gather.3.cloned.1.call-update
  7.3 0.8 select_reduce_fusion.2
  8.5 0.7 add_convert_fusion
  9.5 7.3 %slice.33 = f32[192,256]{1,0:T(8,128)} slice(f32[192,512]{1,0:T(8,128)S(1)} %broadcast_multiply_fusion), slice={[0:192:1], [0:512:2]} | slice | bytes 393216 | tf_op jit(solution)/shard_map/slice | solution.py:22
  16.8 8.1 %gather_fusion = bf16[192,64,512]{2,1,0:T(8,128)(2,1)} fusion(bf16[16,64,512]{2,1,0:T(8,128)(2,1)S(1)} %copy-done.2, s32[1024]{0:T(1024)S(1)} %pad_clamp_fusion.1), kind=kCustom, calls=%fused_computation | custom fusion | bytes 25166592 | tf_op jit(solution)/shard_map/gather | solution.py:89
  24.9 0.7 fusion.49
  25.6 33.9 %all-gather.3.cloned.1.call-done = bf16[192,8192]{1,0:T(8,128)(2,1)} async-done(((bf16[192,512]{1,0:T(8,128)(2,1)}), bf16[192,8192]{1,0:T(8,128)(2,1)}) %all-gather.3.cloned.1.call-update) | async-done | bytes 3145744 | tf_op jit(solution)/shard_map/all_gather | solution.py:72
  59.5 2.6 fusion
  62.1 3.4 convolution_select_fusion
  65.5 59.2 %psum.21 = bf16[192,64]{0,1:T(8,128)(2,1)S(1)} all-reduce(f32[192,64]{0,1:T(8,128)S(1)} %convolution_select_fusion), channel_id=1, replica_groups=mesh['groups'=2,'blk'=16] {'blk'}, use_global_device_ids=true, to_apply=%region_6.7 | all-reduce | flops 12288 | bytes 73728 | tf_op jit(solution)/shard_map/psum | solution.py:88
  124.8 6.5 %fusion.53 = f32[192,1,512]{2,1,0:T(1,128)S(1)} fusion(bf16[192,64,1]{1,2,0:T(2,128)(2,1)S(1)} %copy.109, bf16[192,64,512]{2,1,0:T(8,128)(2,1)} %gather_fusion), kind=kOutput, calls=%fused_computation.118 | convolution fusion | flops 12582912 | bytes 13000704 | tf_op jit(solution)/shard_map/gk,gkq->gq/dot_general | solution.py:90
  131.3 5.3 %convolution_add_fusion = f32[192,512]{1,0:T(8,128)S(1)} fusion(bf16[8192,512]{1,0:T(8,128)(2,1)} %param.14, f32[192,1,512]{2,1,0:T(1,128)S(1)} %fusion.53, bf16[192,8192]{1,0:T(8,128)(2,1)S(1)} %copy-done.5, f32[8192]{0:T(1024)S(1)} %copy-done.11, f32[192]{0:T(256)S(1)} %add_rsqrt_fusion), kind=kOutput, calls=%fused_computation.28 | convolution fusion | flops 1617002496 | bytes 12354304 | tf_op jit(solution)/shard_map/dot_general | solution.py:97
  136.6 6.7 %slice.32 = f32[192,256]{1,0:T(8,128)S(1)} slice(f32[192,512]{1,0:T(8,128)S(1)} %convolution_add_fusion), slice={[0:192:1], [0:512:2]} | slice | bytes 393216 | tf_op jit(solution)/shard_map/slice | solution.py:24
  143.3 6.6 %slice.34 = f32[192,256]{1,0:T(8,128)S(1)} slice(f32[192,512]{1,0:T(8,128)S(1)} %convolution_add_fusion), slice={[0:192:1], [1:512:2]} | slice | bytes 393216 | tf_op jit(solution)/shard_map/slice | solution.py:25
  150.6 0.7 select_convert_fusion
  151.6 12.3 %copy.94 = bf16[16,128,2048]{1,2,0:T(8,128)(2,1)} copy(bf16[16,128,2048]{2,1,0:T(8,128)(2,1)} %param.19) | data formatting | bytes 16777216 | tf_op args[7]
  164.0 1.7 slice.37
  166.4 0.3 fusion.50
  166.7 3.0 fusion.44
  169.8 1.7 slice.36
  171.4 1.7 slice.38
  173.5 22.5 %all_gather.11 = bf16[192,2048]{1,0:T(8,128)(2,1)S(1)} all-gather(bf16[192,128]{1,0:T(8,128)(2,1)S(1)} %select_convert_fusion.1), channel_id=1, replica_groups=mesh['groups'=2,'blk'=16] {'blk'}, dimensions={1}, use_global_device_ids=true | all-gather | bytes 835584 | tf_op jit(solution)/shard_map/all_gather | solution.py:111
  196.2 0.9 fusion.48
  197.1 2.3 all-gather.5.cloned.1.call-done
  199.4 2.8 copy.117
  202.2 1.8 copy-done.3
  204.0 2.3 copy.139
  206.3 2.6 gather_fusion.1
  208.9 3.5 fusion.51
  212.3 0.5 select_reduce_fusion
  213.0 3.7 fusion.52
  216.7 61.5 %pmax.7 = f32[64,8,24]{2,1,0:T(8,128)S(1)} all-reduce(f32[64,8,24]{2,1,0:T(8,128)S(1)} %max.5), channel_id=1, replica_groups=mesh['groups'=2,'blk'=16] {'blk'}, use_global_device_ids=true, to_apply=%region_11.12 | all-reduce | flops 12288 | bytes 98304 | tf_op jit(solution)/shard_map/pmax | solution.py:172
  278.2 0.6 gather_fusion.2
  278.8 4.5 fusion.9
  283.4 3.1 convolution_bitcast_fusion.1
  286.5 6.3 %copy.102 = f32[64,3,8,8,128]{4,3,2,1,0:T(8,128)} copy(f32[64,3,8,8,128]{4,0,3,1,2:T(8,128)S(1)} %convolution_bitcast_fusion.1) | data formatting | bytes 12582912 | tf_op jit(solution)/shard_map/transpose | solution.py:54
  292.8 7.2 %reshape.302 = f32[192,8192]{1,0:T(8,128)} reshape(f32[64,3,8,8,128]{4,3,2,1,0:T(8,128)} %copy.102) | data formatting | bytes 12582912 | tf_op jit(solution)/shard_map/reshape | solution.py:54
  300.0 1.8 convolution_bitcast_fusion
  301.8 3.3 copy.138
  305.1 7.4 %reshape.304 = f32[192,8192]{1,0:T(8,128)} reshape(f32[64,3,8,8,128]{4,3,2,1,0:T(8,128)} %bitcast.122) | data formatting | bytes 12582912 | tf_op jit(solution)/shard_map/reshape | solution.py:54
  312.6 0.9 fusion.21
  313.7 0.3 copy.108
  314.3 0.9 fusion.11
  316.0 61.4 %psum.23 = f32[192,64]{1,0:T(8,128)S(1)} all-reduce(f32[192,64]{1,0:T(8,128)S(1)} %reshape.306), channel_id=1, replica_groups=mesh['groups'=2,'blk'=16] {'blk'}, use_global_device_ids=true, to_apply=%region_14.15 | all-reduce | flops 12288 | bytes 98304 | tf_op jit(solution)/shard_map/psum | solution.py:197
  377.4 60.1 %all-reduce.2.cloned.1.call-done = f32[192,8192]{1,0:T(8,128)} async-done(((f32[192,8192]{1,0:T(8,128)}), f32[192,8192]{1,0:T(8,128)}) %all-reduce.2.cloned.1.call-update) | async-done | bytes 6291472 | tf_op jit(solution)/shard_map/psum | solution.py:197
  437.5 1.8 broadcast_in_dim.194
  439.3 1.0 copy-done.4
  440.3 10.9 %fusion.13 = bf16[192,512]{1,0:T(8,128)(2,1)} fusion(bf16[8192,512]{1,0:T(8,128)(2,1)} %param.16, f32[24,8,64,128]{3,2,1,0:T(8,128)S(1)} %bitcast.125, f32[192,8192]{1,0:T(8,128)} %all-reduce.2.cloned.1.call-done, f32[192,8192]{1,0:T(8,128)S(1)} %copy-done.4), kind=kOutput, calls=%fused_computation.29 | convolution fusion | flops 1615429632 | bytes 27459584 | tf_op jit(solution)/shard_map/dot_general | solution.py:202
  (74 shorter events, 4.5 us)
Async XLA Ops:
  6.5 160.2 %copy-start = (bf16[8192,128]{1,0:T(8,128)(2,1)S(1)}, bf16[8192,128]{1,0:T(8,128)(2,1)}, u32[]{:S(2)}) copy-start(bf16[8192,128]{1,0:T(8,128)(2,1)} %param.15) | copy-start | bytes 6291460
  6.5 10.3 %copy-start.2 = (bf16[16,64,512]{2,1,0:T(8,128)(2,1)S(1)}, bf16[16,64,512]{2,1,0:T(8,128)(2,1)}, u32[]{:S(2)}) copy-start(bf16[16,64,512]{2,1,0:T(8,128)(2,1)} %param.18) | copy-start | bytes 3145732
  6.5 52.9 %all-gather.3.cloned.1.call-start = ((), (), s32[]{:S(2)}) async-start(), calls=%async_computation | async-start | bytes 3342336 | tf_op jit(solution)/shard_map/all_gather | solution.py:72
  7.3 192.2 %all-gather.5.cloned.1.call-start = ((), (), s32[]{:S(2)}) async-start(), calls=%async_computation.1 | async-start | bytes 3342336 | tf_op jit(solution)/shard_map/all_gather | solution.py:110
  16.8 8.1 %copy-start.6 = (f32[192,256]{1,0:T(8,128)S(1)}, f32[192,256]{1,0:T(8,128)}, u32[]{:S(2)}) copy-start(f32[192,256]{1,0:T(8,128)} %slice.33) | copy-start | bytes 589828
  124.8 6.5 %copy-start.5 = (bf16[192,8192]{1,0:T(8,128)(2,1)S(1)}, bf16[192,8192]{1,0:T(8,128)(2,1)}, u32[]{:S(2)}) copy-start(bf16[192,8192]{1,0:T(8,128)(2,1)} %all-gather.3.cloned.1.call-done) | copy-start | bytes 9437188
  124.8 6.5 %copy-start.11 = (f32[8192]{0:T(1024)S(1)}, f32[8192]{0:T(1024)}, u32[]{:S(2)}) copy-start(f32[8192]{0:T(1024)} %param.13) | copy-start | bytes 98308
  151.3 286.2 %all-reduce.2.cloned.1.call-start = ((), (), s32[]{:S(2)}) async-start(), calls=%async_computation.2 | async-start | bytes 12582912 | tf_op jit(solution)/shard_map/psum | solution.py:197
  151.6 14.2 %copy-start.9 = (s32[64,4]{0,1:T(4,128)S(1)}, s32[64,4]{0,1:T(4,128)}, u32[]{:S(2)}) copy-start(s32[64,4]{0,1:T(4,128)} %param.23) | copy-start | bytes 3076
  151.6 14.3 %copy-start.10 = (s32[64]{0:T(128)S(1)}, s32[64]{0:T(128)}, u32[]{:S(2)}) copy-start(s32[64]{0:T(128)} %param.22) | copy-start | bytes 772
  202.2 1.8 copy-start.3
  278.8 7.7 %copy-start.7 = (f32[16,8,24]{2,1,0:T(8,128)}, f32[16,8,24]{2,1,0:T(8,128)S(1)}, u32[]{:S(2)}) copy-start(f32[16,8,24]{2,1,0:T(8,128)S(1)} %gather_fusion.2) | copy-start | bytes 36868
  305.1 9.1 %copy-start.8 = (f32[16,8,24]{2,1,0:T(8,128)S(1)}, f32[16,8,24]{2,1,0:T(8,128)}, u32[]{:S(2)}) copy-start(f32[16,8,24]{2,1,0:T(8,128)} %copy-done.7) | copy-start | bytes 36868
  437.5 2.8 copy-start.4
  440.3 10.9 %copy-start.1 = (bf16[8192,128]{1,0:T(8,128)(2,1)S(1)}, bf16[8192,128]{1,0:T(8,128)(2,1)}, u32[]{:S(2)}) copy-start(bf16[8192,128]{1,0:T(8,128)(2,1)} %param.15) | copy-start | bytes 6291460
Sparse Core Ops, SparseCore 0:
  9.5 49.8 all-gather.2
  151.4 47.9 all-gather.4
  300.1 137.3 all-reduce.1
where the time goes:
time: 464 us; the launch traced here: 458 us
  blocking collectives  205 us (44%)
  waiting for transfers between devices  97 us (21%)
  local copies, waits for them, and re-layouts  88.1 us (19%)
  matrix products  45.9 us (10%)
  between operations  13.7 us (3%)
  other arithmetic  8.25 us (2%)
    pmax x1, blocking collectives, local(): lax.pmax(jnp.maximum(req_peak, jnp.max(fresh_masked, axis=-1)), 'blk')  61.5 us
    psum x1, blocking collectives, local(): num_all, den_all = lax.psum((num_tok, den_tok), 'blk')  61.4 us
    psum x1, waiting for transfers between devices, local(): num_all, den_all = lax.psum((num_tok, den_tok), 'blk')  60.1 us
    psum x1, blocking collectives, local(): adapter_choice_index = lax.psum(partial_codes, 'blk').astype(jnp.bfloat16)  59.2 us
    all_gather x1, waiting for transfers between devices, local(): gathered = lax.all_gather(layer_input_tokens, 'blk', axis=1, tiled=True)  33.9 us
    all_gather x1, blocking collectives, local(): lax.all_gather(keyval_part, 'blk', axis=1, tiled=True)  22.5 us
    unnamed x27, local copies, waits for them, and re-layouts  18 us
    reshape x4, local copies, waits for them, and re-layouts, to_tokens(): split_head_shape.transpose(order_axes)  15.1 us
  transfers between devices with their start and end apart: 3, of which 3 were waited for; matrix products, arithmetic and copies ran while one was open for 12% of the time, Pallas kernels for 0%

commit v1 on v0

--- a/solution.py
+++ b/solution.py
@@ -85,7 +85,9 @@
         "ly,mxy->lmx", normalized_input, adapter_down_weight, preferred_element_type=jnp.float32
     )
     partial_codes = jnp.sum(jnp.where(local_pick[:, :, None], output_projected, 0.0), axis=1)
-    adapter_choice_index = lax.psum(partial_codes, "blk").astype(jnp.bfloat16)
+    adapter_choice_index = jnp.sum(lax.all_gather(partial_codes, "blk"), axis=0).astype(
+        jnp.bfloat16
+    )
     up_weight_rows = adapter_up_weight[token_cache_slot]
     adapter_query_update = jnp.einsum(
         "gk,gkq->gq", adapter_choice_index, up_weight_rows, preferred_element_type=jnp.float32

time: 464 us -> 430 us (0.927)
  blocking collectives: 205 us -> 169 us
    psum x1 -> x0, blocking collectives: 59.2 us -> none  [local(): adapter_choice_index = lax.psum(partial_codes, 'blk').astype(jnp.bfloat16)]
    all_gather x0 -> x1, blocking collectives: none -> 21.8 us  [local(): lax.all_gather(partial_codes, 'blk')]
    unnamed x27 -> x29, local copies, waits for them, and re-layouts: 18 us -> 18 us
  transfers between devices with their start and end apart: 3 -> 3, of which waited for: 3 -> 3; matrix products, arithmetic and copies ran while one was open for 12% -> 14% of each run, Pallas kernels for 0% -> 0%
where the time goes in v1:
time: 430 us; the launch traced here: 423 us
  blocking collectives  169 us (39%)
  waiting for transfers between devices  96.8 us (23%)
  local copies, waits for them, and re-layouts  88.8 us (21%)
  matrix products  46 us (11%)
  between operations  13.8 us (3%)
  other arithmetic  8.31 us (2%)
    pmax x1, blocking collectives, local(): lax.pmax(jnp.maximum(req_peak, jnp.max(fresh_masked, axis=-1)), 'blk')  62.8 us
    psum x1, blocking collectives, local(): num_all, den_all = lax.psum((num_tok, den_tok), 'blk')  61.3 us
    psum x1, waiting for transfers between devices, local(): num_all, den_all = lax.psum((num_tok, den_tok), 'blk')  60.1 us
    all_gather x1, waiting for transfers between devices, local(): gathered = lax.all_gather(layer_input_tokens, 'blk', axis=1, tiled=True)  33.2 us
    all_gather x1, blocking collectives, local(): lax.all_gather(keyval_part, 'blk', axis=1, tiled=True)  23.6 us
    all_gather x1, blocking collectives, local(): lax.all_gather(partial_codes, 'blk')  21.8 us
    unnamed x29, local copies, waits for them, and re-layouts  18 us
    reshape x4, local copies, waits for them, and re-layouts, to_tokens(): split_head_shape.transpose(order_axes)  15.1 us
  transfers between devices with their start and end apart: 3, of which 3 were waited for; matrix products, arithmetic and copies ran while one was open for 14% of the time, Pallas kernels for 0%

profile of v1, /device:TPU:0, one launch (start us, length us, event | category | flops | bytes accessed | tf_op | source)
XLA Modules:
  0.0 423.3 jit_solution(4636294581598989073)
XLA Ops:
  6.5 0.7 all-gather.5.cloned.1.call-update
  7.3 0.8 select_reduce_fusion.2
  8.5 0.7 add_convert_fusion
  9.5 7.3 %slice.33 = f32[192,256]{1,0:T(8,128)} slice(f32[192,512]{1,0:T(8,128)S(1)} %broadcast_multiply_fusion), slice={[0:192:1], [0:512:2]} | slice | bytes 393216 | tf_op jit(solution)/shard_map/slice | solution.py:22
  16.8 8.1 %gather_fusion = bf16[192,64,512]{2,1,0:T(8,128)(2,1)} fusion(bf16[16,64,512]{2,1,0:T(8,128)(2,1)S(1)} %copy-done.2, s32[1024]{0:T(1024)S(1)} %pad_clamp_fusion.1), kind=kCustom, calls=%fused_computation | custom fusion | bytes 25166592 | tf_op jit(solution)/shard_map/gather | solution.py:91
  24.9 1.4 fusion.50
  26.3 33.2 %all-gather.5.cloned.1.call-done = bf16[192,8192]{1,0:T(8,128)(2,1)} async-done(((bf16[192,512]{1,0:T(8,128)(2,1)}), bf16[192,8192]{1,0:T(8,128)(2,1)}) %all-gather.5.cloned.1.call-update) | async-done | bytes 3145744 | tf_op jit(solution)/shard_map/all_gather | solution.py:72
  59.5 2.6 fusion
  62.1 3.4 fusion.16
  65.5 21.8 %all-gather.1 = f32[16,192,64]{1,2,0:T(8,128)S(1)} all-gather(f32[1,192,64]{1,2,0:T(8,128)S(1)} %fusion.16), channel_id=2, replica_groups=mesh['groups'=2,'blk'=16] {'blk'}, dimensions={0}, use_global_device_ids=true | all-gather | bytes 835584 | tf_op jit(solution)/shard_map/all_gather | solution.py:88
  87.5 6.5 %fusion.54 = f32[192,1,512]{2,1,0:T(1,128)S(1)} fusion(bf16[192,64,1]{1,2,0:T(2,128)(2,1)S(1)} %copy.109, bf16[192,64,512]{2,1,0:T(8,128)(2,1)} %gather_fusion), kind=kOutput, calls=%fused_computation.119 | convolution fusion | flops 12582912 | bytes 13000704 | tf_op jit(solution)/shard_map/gk,gkq->gq/dot_general | solution.py:92
  93.9 5.4 %convolution_add_fusion = f32[192,512]{1,0:T(8,128)S(1)} fusion(bf16[8192,512]{1,0:T(8,128)(2,1)} %param.14, f32[192,1,512]{2,1,0:T(1,128)S(1)} %fusion.54, bf16[192,8192]{1,0:T(8,128)(2,1)S(1)} %copy-done.5, f32[8192]{0:T(1024)S(1)} %copy-done.12, f32[192]{0:T(256)S(1)} %add_rsqrt_fusion), kind=kOutput, calls=%fused_computation.28 | convolution fusion | flops 1617002496 | bytes 12354304 | tf_op jit(solution)/shard_map/dot_general | solution.py:99
  99.3 6.7 %slice.32 = f32[192,256]{1,0:T(8,128)S(1)} slice(f32[192,512]{1,0:T(8,128)S(1)} %convolution_add_fusion), slice={[0:192:1], [0:512:2]} | slice | bytes 393216 | tf_op jit(solution)/shard_map/slice | solution.py:24
  106.0 6.6 %slice.34 = f32[192,256]{1,0:T(8,128)S(1)} slice(f32[192,512]{1,0:T(8,128)S(1)} %convolution_add_fusion), slice={[0:192:1], [1:512:2]} | slice | bytes 393216 | tf_op jit(solution)/shard_map/slice | solution.py:25
  113.3 0.7 select_convert_fusion
  114.3 12.3 %copy.94 = bf16[16,128,2048]{1,2,0:T(8,128)(2,1)} copy(bf16[16,128,2048]{2,1,0:T(8,128)(2,1)} %param.19) | data formatting | bytes 16777216 | tf_op args[7]
  126.7 1.7 slice.37
  129.1 0.3 fusion.51
  129.4 3.0 fusion.45
  132.4 1.7 slice.36
  134.1 1.7 slice.38
  136.2 23.6 %all_gather.19 = bf16[192,2048]{1,0:T(8,128)(2,1)S(1)} all-gather(bf16[192,128]{1,0:T(8,128)(2,1)S(1)} %select_convert_fusion.1), channel_id=1, replica_groups=mesh['groups'=2,'blk'=16] {'blk'}, dimensions={1}, use_global_device_ids=true | all-gather | bytes 835584 | tf_op jit(solution)/shard_map/all_gather | solution.py:113
  160.0 0.9 fusion.49
  160.9 2.7 all-gather.7.cloned.1.call-done
  163.6 2.8 copy.117
  166.4 1.8 copy-done.3
  168.2 2.3 copy.139
  170.5 2.6 gather_fusion.1
  173.1 3.5 fusion.52
  176.5 0.5 select_reduce_fusion
  177.2 3.7 fusion.53
  180.9 62.8 %pmax.7 = f32[64,8,24]{2,1,0:T(8,128)S(1)} all-reduce(f32[64,8,24]{2,1,0:T(8,128)S(1)} %max.5), channel_id=1, replica_groups=mesh['groups'=2,'blk'=16] {'blk'}, use_global_device_ids=true, to_apply=%region_11.12 | all-reduce | flops 12288 | bytes 98304 | tf_op jit(solution)/shard_map/pmax | solution.py:174
  243.7 0.6 gather_fusion.2
  244.3 4.5 %fusion.9 = f32[8,3,8,128,16]{3,2,1,0,4:T(8,128)S(1)} fusion(bf16[16,128,2,8,128]{1,4,3,2,0:T(8,128)(2,1)} %bitcast.123, f32[16,8,24,128]{3,2,1,0:T(8,128)S(1)} %get-tuple-element.20, f32[16,8,24]{2,1,0:T(8,128)S(1)} %gather_fusion.2, pred[16,128]{1,0:T(8,128)(4,1)S(1)} %fusion.30), kind=kOutput, calls=%fused_computation.23 | convolution fusion | flops 101842944 | bytes 7354368 | tf_op jit(solution)/shard_map/skqp,spkd->skqd/dot_general | solution.py:176
  248.8 3.1 convolution_bitcast_fusion.1
  251.9 6.3 %copy.102 = f32[64,3,8,8,128]{4,3,2,1,0:T(8,128)} copy(f32[64,3,8,8,128]{4,0,3,1,2:T(8,128)S(1)} %convolution_bitcast_fusion.1) | data formatting | bytes 12582912 | tf_op jit(solution)/shard_map/transpose | solution.py:54
  258.2 7.2 %reshape.303 = f32[192,8192]{1,0:T(8,128)} reshape(f32[64,3,8,8,128]{4,3,2,1,0:T(8,128)} %copy.102) | data formatting | bytes 12582912 | tf_op jit(solution)/shard_map/reshape | solution.py:54
  265.4 1.8 convolution_bitcast_fusion
  267.3 3.3 copy.138
  270.6 7.4 %reshape.305 = f32[192,8192]{1,0:T(8,128)} reshape(f32[64,3,8,8,128]{4,3,2,1,0:T(8,128)} %bitcast.124) | data formatting | bytes 12582912 | tf_op jit(solution)/shard_map/reshape | solution.py:54
  278.0 0.9 fusion.22
  279.1 0.3 copy.108
  279.7 0.9 fusion.11
  281.5 61.3 %psum.15 = f32[192,64]{1,0:T(8,128)S(1)} all-reduce(f32[192,64]{1,0:T(8,128)S(1)} %reshape.307), channel_id=1, replica_groups=mesh['groups'=2,'blk'=16] {'blk'}, use_global_device_ids=true, to_apply=%region_14.15 | all-reduce | flops 12288 | bytes 98304 | tf_op jit(solution)/shard_map/psum | solution.py:199
  342.8 60.1 %all-reduce.2.cloned.1.call-done = f32[192,8192]{1,0:T(8,128)} async-done(((f32[192,8192]{1,0:T(8,128)}), f32[192,8192]{1,0:T(8,128)}) %all-reduce.2.cloned.1.call-update) | async-done | bytes 6291472 | tf_op jit(solution)/shard_map/psum | solution.py:199
  402.9 1.8 broadcast_in_dim.194
  404.7 1.0 copy-done.4
  405.7 10.9 %fusion.13 = bf16[192,512]{1,0:T(8,128)(2,1)} fusion(bf16[8192,512]{1,0:T(8,128)(2,1)} %param.16, f32[24,8,64,128]{3,2,1,0:T(8,128)S(1)} %bitcast.127, f32[192,8192]{1,0:T(8,128)} %all-reduce.2.cloned.1.call-done, f32[192,8192]{1,0:T(8,128)S(1)} %copy-done.4), kind=kOutput, calls=%fused_computation.29 | convolution fusion | flops 1615429632 | bytes 27459584 | tf_op jit(solution)/shard_map/dot_general | solution.py:204
  (77 shorter events, 4.6 us)
Async XLA Ops:
  6.5 122.9 %copy-start = (bf16[8192,128]{1,0:T(8,128)(2,1)S(1)}, bf16[8192,128]{1,0:T(8,128)(2,1)}, u32[]{:S(2)}) copy-start(bf16[8192,128]{1,0:T(8,128)(2,1)} %param.15) | copy-start | bytes 6291460
  6.5 10.3 %copy-start.2 = (bf16[16,64,512]{2,1,0:T(8,128)(2,1)S(1)}, bf16[16,64,512]{2,1,0:T(8,128)(2,1)}, u32[]{:S(2)}) copy-start(bf16[16,64,512]{2,1,0:T(8,128)(2,1)} %param.18) | copy-start | bytes 3145732
  6.5 52.9 %all-gather.5.cloned.1.call-start = ((), (), s32[]{:S(2)}) async-start(), calls=%async_computation | async-start | bytes 3342336 | tf_op jit(solution)/shard_map/all_gather | solution.py:72
  7.3 156.4 %all-gather.7.cloned.1.call-start = ((), (), s32[]{:S(2)}) async-start(), calls=%async_computation.1 | async-start | bytes 3342336 | tf_op jit(solution)/shard_map/all_gather | solution.py:112
  16.8 8.1 %copy-start.6 = (f32[192,256]{1,0:T(8,128)S(1)}, f32[192,256]{1,0:T(8,128)}, u32[]{:S(2)}) copy-start(f32[192,256]{1,0:T(8,128)} %slice.33) | copy-start | bytes 589828
  87.4 6.5 %copy-start.5 = (bf16[192,8192]{1,0:T(8,128)(2,1)S(1)}, bf16[192,8192]{1,0:T(8,128)(2,1)}, u32[]{:S(2)}) copy-start(bf16[192,8192]{1,0:T(8,128)(2,1)} %all-gather.5.cloned.1.call-done) | copy-start | bytes 9437188
  87.4 6.5 %copy-start.12 = (f32[8192]{0:T(1024)S(1)}, f32[8192]{0:T(1024)}, u32[]{:S(2)}) copy-start(f32[8192]{0:T(1024)} %param.13) | copy-start | bytes 98308
  93.9 18.7 %copy-start.7 = (f32[192,256]{1,0:T(8,128)S(1)}, f32[192,256]{1,0:T(8,128)}, u32[]{:S(2)}) copy-start(f32[192,256]{1,0:T(8,128)} %get-tuple-element.16) | copy-start | bytes 589828
  114.0 288.9 %all-reduce.2.cloned.1.call-start = ((), (), s32[]{:S(2)}) async-start(), calls=%async_computation.2 | async-start | bytes 12582912 | tf_op jit(solution)/shard_map/psum | solution.py:199
  114.3 14.2 %copy-start.10 = (s32[64,4]{0,1:T(4,128)S(1)}, s32[64,4]{0,1:T(4,128)}, u32[]{:S(2)}) copy-start(s32[64,4]{0,1:T(4,128)} %param.23) | copy-start | bytes 3076
  114.3 14.3 %copy-start.11 = (s32[64]{0:T(128)S(1)}, s32[64]{0:T(128)}, u32[]{:S(2)}) copy-start(s32[64]{0:T(128)} %param.22) | copy-start | bytes 772
  166.4 1.8 copy-start.3
  244.3 7.7 %copy-start.8 = (f32[16,8,24]{2,1,0:T(8,128)}, f32[16,8,24]{2,1,0:T(8,128)S(1)}, u32[]{:S(2)}) copy-start(f32[16,8,24]{2,1,0:T(8,128)S(1)} %gather_fusion.2) | copy-start | bytes 36868
  270.6 9.1 %copy-start.9 = (f32[16,8,24]{2,1,0:T(8,128)S(1)}, f32[16,8,24]{2,1,0:T(8,128)}, u32[]{:S(2)}) copy-start(f32[16,8,24]{2,1,0:T(8,128)} %copy-done.8) | copy-start | bytes 36868
  402.9 2.8 copy-start.4
  405.7 10.9 %copy-start.1 = (bf16[8192,128]{1,0:T(8,128)(2,1)S(1)}, bf16[8192,128]{1,0:T(8,128)(2,1)}, u32[]{:S(2)}) copy-start(bf16[8192,128]{1,0:T(8,128)(2,1)} %param.15) | copy-start | bytes 6291460
Sparse Core Ops, SparseCore 0:
  9.5 49.8 all-gather.4
  114.2 49.4 all-gather.6
  265.5 137.3 all-reduce.1
